TPU v7x, 256 devices: a whole 4x4x8 slice. The times are simulated.
256 devices in a mesh: gx: 32 (over z, y), gy: 4 (over x), gz: 2 (over core).
Axes of the slice: x: 4, y: 4, z: 8, core: 2. Of those that a mesh axis runs over, the one named last changes fastest.
Arguments:
- mass_per_volume: float32 [16, 512, 512], P('gz', 'gx', 'gy'), may hold values from 0.5 to 2
- flow_speed: float32 [3, 16, 512, 512], P(None, 'gz', 'gx', 'gy'), may hold values from -3 to 3
- pressure: float32 [16, 512, 512], P('gz', 'gx', 'gy'), may hold values from 0.5 to 2
- cotangent: float32 [5, 16, 512, 512], P(None, 'gz', 'gx', 'gy'), may hold values from -6 to 6
- weight_inner: float32 [64, 9], replicated, may hold values from -2 to 2
- weight_middle: float32 [64, 64], replicated, may hold values from -0.75 to 0.75
- weight_outer: float32 [64], replicated, may hold values from -0.75 to 0.75
Outputs:
- state_next: float32 [5, 16, 512, 512], P(None, 'gz', 'gx', 'gy')
- adjoint_density: float32 [16, 512, 512], P('gz', 'gx', 'gy')
- adjoint_velocity: float32 [3, 16, 512, 512], P(None, 'gz', 'gx', 'gy')
- adjoint_pressure: float32 [16, 512, 512], P('gz', 'gx', 'gy')
- adjoint_inner: float32 [64, 9], replicated
- adjoint_middle: float32 [64, 64], replicated
- adjoint_outer: float32 [64], replicated
All inputs are finite; a program needn't handle non-finite values.
Results may differ from a plain program's by a relative error of at most 0.0003.
Values sent between devices are 32-bit elements; how exact they have to be, the bound alone decides.
No kernel may reach another device: no remote copies, remote signals or barrier semaphores. Data moves between devices by JAX's collectives and lax.ppermute only.
A program may use at most 64 MiB of HBM per device.

v0:
```python
import math

import jax
import jax.numpy as jnp
import numpy as np
from jax import lax
from jax.experimental import pallas as pl
from jax.experimental.pallas import tpu as pltpu
from jax.sharding import PartitionSpec as P

HEAT_RATIO = 1.4
THERMAL_DIFFUSE = 3.5
EDDY_SCALE = 0.5
TIME_STEP = 0.1
COMPACT_ALPHA = 1.0 / 3.0
COMPACT_NEAR = 14.0 / 9.0
COMPACT_FAR = 1.0 / 9.0
HIGHEST_PRECISION = lax.Precision.HIGHEST
NEAR_HALO = 2
NETWORK_PRECISION = lax.Precision.HIGH
NETWORK_BLOCK = 2048


def from_behind(value, axis, steps):
    count = lax.axis_size(axis)
    pairs = [(source, (source + steps) % count) for source in range(count)]
    return lax.ppermute(value, axis, pairs)


def prepare(mass_per_volume, flow_speed, pressure):
    energy = pressure / (HEAT_RATIO - 1.0) + 0.5 * mass_per_volume * jnp.sum(
        flow_speed * flow_speed, 0
    )
    state_now = jnp.concatenate(
        [mass_per_volume[None], mass_per_volume[None] * flow_speed, energy[None]], 0
    )
    scalars = jnp.concatenate([flow_speed, (pressure / mass_per_volume)[None]], 0)
    return (state_now, scalars)


def fluxes(mass_per_volume, flow_speed, pressure, upstream_cotangent, eddy_viscosity):
    energy = pressure / (HEAT_RATIO - 1.0) + 0.5 * mass_per_volume * jnp.sum(
        flow_speed * flow_speed, 0
    )
    attenuation_coefficient = mass_per_volume * eddy_viscosity
    stagnation_specific_energy = energy + pressure
    directions = []
    for traversal_axis in range(3):
        transported_array = flow_speed[traversal_axis]
        partition_parts = [mass_per_volume * transported_array]
        for coordinate_slot in range(3):
            mass_flux_array = (
                mass_per_volume * flow_speed[coordinate_slot] * transported_array
                - attenuation_coefficient * upstream_cotangent[traversal_axis, coordinate_slot]
            )
            if coordinate_slot == traversal_axis:
                mass_flux_array = mass_flux_array + pressure
            partition_parts.append(mass_flux_array)
        partition_parts.append(
            stagnation_specific_energy * transported_array
            - THERMAL_DIFFUSE * attenuation_coefficient * upstream_cotangent[traversal_axis, 3]
        )
        directions.append(jnp.stack(partition_parts))
    return jnp.stack(directions)


def viscosity(upstream_cotangent, inner_weight, middle_weight, outer_weight):
    features = upstream_cotangent[:, :3].reshape((9,) + upstream_cotangent.shape[2:])
    hidden = jnp.tanh(
        jnp.einsum("hc,czxy->hzxy", inner_weight, features, precision=NETWORK_PRECISION)
    )
    hidden = jnp.tanh(
        jnp.einsum("hk,kzxy->hzxy", middle_weight, hidden, precision=NETWORK_PRECISION)
    )
    output = jnp.einsum("h,hzxy->zxy", outer_weight, hidden, precision=NETWORK_PRECISION)
    return EDDY_SCALE * jax.nn.softplus(output)


def local_flux(
    density_in, velocity_in, pressure_in, upstream_cotangent, inner_in, middle_in, outer_in
):
    eddy_viscosity = viscosity(upstream_cotangent, inner_in, middle_in, outer_in)
    return fluxes(density_in, velocity_in, pressure_in, upstream_cotangent, eddy_viscosity)


def network_kernel(
    features_ref, eddy_bar_ref, inner_ref, inner_t_ref, middle_ref, middle_t_ref, outer_ref,
    eddy_ref, features_bar_ref, inner_bar_ref, middle_bar_ref, outer_bar_ref,
):
    exact = lax.Precision.HIGHEST
    features = features_ref[...]
    first = jnp.tanh(jnp.dot(inner_ref[...], features, precision=exact))
    second = jnp.tanh(jnp.dot(middle_ref[...], first, precision=exact))
    output = jnp.sum(outer_ref[...] * second, axis=0, keepdims=True)
    soft = jnp.maximum(output, 0.0) + jnp.log1p(jnp.exp(-jnp.abs(output)))
    eddy_ref[...] = EDDY_SCALE * soft
    output_bar = EDDY_SCALE * eddy_bar_ref[...] / (1.0 + jnp.exp(-output))
    second_pre_bar = outer_ref[...] * output_bar * (1.0 - second * second)
    first_pre_bar = jnp.dot(middle_t_ref[...], second_pre_bar, precision=exact) * (
        1.0 - first * first
    )
    features_bar_ref[...] = jnp.dot(inner_t_ref[...], first_pre_bar, precision=exact)
    by_cells = (((1,), (1,)), ((), ()))
    middle_part = lax.dot_general(second_pre_bar, first, by_cells, precision=exact)
    inner_part = lax.dot_general(first_pre_bar, features, by_cells, precision=exact)
    outer_part = jnp.sum(second * output_bar, axis=1, keepdims=True)

    @pl.when(pl.program_id(0) == 0)
    def _():
        inner_bar_ref[...] = jnp.zeros_like(inner_bar_ref)
        middle_bar_ref[...] = jnp.zeros_like(middle_bar_ref)
        outer_bar_ref[...] = jnp.zeros_like(outer_bar_ref)

    inner_bar_ref[...] += inner_part
    middle_bar_ref[...] += middle_part
    outer_bar_ref[...] += outer_part


def network(features, eddy_bar, inner_weight, middle_weight, outer_weight):
    inputs, cells = features.shape
    hidden = inner_weight.shape[0]
    block = min(NETWORK_BLOCK, cells)
    outer_column = outer_weight.reshape(hidden, 1)

    def whole(shape):
        return pl.BlockSpec(shape, lambda i: (0, 0))

    def lanes(rows):
        return pl.BlockSpec((rows, block), lambda i: (0, i))

    return pl.pallas_call(
        network_kernel,
        grid=(cells // block,),
        in_specs=[
            lanes(inputs),
            lanes(1),
            whole((hidden, inputs)),
            whole((inputs, hidden)),
            whole((hidden, hidden)),
            whole((hidden, hidden)),
            whole((hidden, 1)),
        ],
        out_specs=[
            lanes(1),
            lanes(inputs),
            whole((hidden, inputs)),
            whole((hidden, hidden)),
            whole((hidden, 1)),
        ],
        out_shape=[
            jax.ShapeDtypeStruct((1, cells), jnp.float32),
            jax.ShapeDtypeStruct((inputs, cells), jnp.float32),
            jax.ShapeDtypeStruct((hidden, inputs), jnp.float32),
            jax.ShapeDtypeStruct((hidden, hidden), jnp.float32),
            jax.ShapeDtypeStruct((hidden, 1), jnp.float32),
        ],
        compiler_params=pltpu.CompilerParams(dimension_semantics=("arbitrary",)),
    )(features, eddy_bar, inner_weight, inner_weight.T, middle_weight, middle_weight.T, outer_column)


def compact_tables(x_cells, line_length):
    eye = np.eye(line_length)
    system = eye + COMPACT_ALPHA * (np.roll(eye, 1, 1) + np.roll(eye, -1, 1))
    right = np.zeros((line_length, line_length))
    cells = np.arange(line_length)
    for offset, value in (
        (1, 0.5 * COMPACT_NEAR),
        (-1, -0.5 * COMPACT_NEAR),
        (2, 0.25 * COMPACT_FAR),
        (-2, -0.25 * COMPACT_FAR),
    ):
        right[cells, (cells + offset) % line_length] += value
    row = np.linalg.solve(system, right)[0]

    def coef(offset):
        return row[offset % line_length]

    ratio = (-1.0 + np.sqrt(1.0 - 4.0 * COMPACT_ALPHA**2)) / (2.0 * COMPACT_ALPHA)
    gain = coef(NEAR_HALO + 1) / ratio ** (NEAR_HALO + 1)
    n, h = x_cells, NEAR_HALO
    own = np.arange(n)
    send = np.zeros((2 * h + 4, n))
    for k in range(h):
        send[k, n - h + k] = 1.0
    send[h, : n - h] = ratio ** (n - own[: n - h])
    send[h + 1] = ratio ** (2 * n - own)
    for k in range(h):
        send[h + 2 + k, k] = 1.0
    send[2 * h + 2, h:] = ratio ** own[h:]
    send[2 * h + 3] = ratio ** (n + own)
    width = n + 2 * h + 4
    take = np.zeros((n, width))
    for i in range(n):
        take[i, 0] = -gain * ratio**i
        for k in range(h):
            take[i, 1 + k] = coef(-h + k - i)
        take[i, 1 + h] = -gain * ratio**i
        for m in range(n):
            take[i, 2 + h + m] = coef(m - i)
        for k in range(h):
            take[i, 2 + h + n + k] = coef(n + k - i)
        take[i, 2 + 2 * h + n] = gain * ratio ** (n - i)
        take[i, 3 + 2 * h + n] = gain * ratio ** (n - i)
    return send, take


def derive_x(fields):
    x_cells = fields.shape[2]
    groups = lax.axis_size("gx")
    h = NEAR_HALO
    send, take = compact_tables(x_cells, x_cells * groups)
    send = jnp.asarray(send, jnp.float32)
    take = jnp.asarray(take, jnp.float32)
    planes = jnp.einsum("pj,fzjy->fzpy", send, fields, precision=HIGHEST_PRECISION)
    to_right = planes[:, :, : h + 1]
    to_right2 = planes[:, :, h + 1 : h + 2]
    to_left = planes[:, :, h + 2 : 2 * h + 3]
    to_left2 = planes[:, :, 2 * h + 3 :]
    from_left = from_behind(to_right, "gx", 1)
    from_left2 = from_behind(to_right2, "gx", 2)
    from_right = from_behind(to_left, "gx", -1)
    from_right2 = from_behind(to_left2, "gx", -2)
    received = jnp.concatenate([from_left2, from_left, from_right, from_right2], axis=2)
    take_own = take[:, h + 2 : h + 2 + x_cells]
    take_received = jnp.concatenate([take[:, : h + 2], take[:, h + 2 + x_cells :]], axis=1)
    own_part = jnp.einsum("ij,fzjy->fziy", take_own, fields, precision=HIGHEST_PRECISION)
    return own_part + jnp.einsum(
        "ij,fzjy->fziy", take_received, received, precision=HIGHEST_PRECISION
    )


def halo(block, axis, dim, width):
    count = lax.axis_size(axis)
    size = block.shape[dim]
    low_part = lax.slice_in_dim(block, size - width, size, axis=dim)
    high_part = lax.slice_in_dim(block, 0, width, axis=dim)
    if count == 2:
        both = from_behind(jnp.concatenate([low_part, high_part], axis=dim), axis, 1)
        low = lax.slice_in_dim(both, 0, width, axis=dim)
        high = lax.slice_in_dim(both, width, 2 * width, axis=dim)
    else:
        low = from_behind(low_part, axis, 1)
        high = from_behind(high_part, axis, -1)
    return jnp.concatenate([low, block, high], axis=dim)


def centered(extended, along_axis, margin, length):

    def shifted(offset):
        return lax.slice_in_dim(
            extended, margin + offset, margin + offset + length, axis=along_axis
        )

    return (
        45.0 * (shifted(1) - shifted(-1))
        - 9.0 * (shifted(2) - shifted(-2))
        + (shifted(3) - shifted(-3))
    ) / 60.0


def derive_y(fields):
    return centered(halo(fields, "gy", 3, 3), 3, 3, fields.shape[3])


def derive_z(fields):
    return centered(halo(fields, "gz", 1, 3), 1, 3, fields.shape[1])


def butterfly_sum(value, axis):
    count = lax.axis_size(axis)
    step = 1
    while step < count:
        if count % (2 * step) == 0:
            pairs = [(s, s ^ step) for s in range(count)]
            value = value + lax.ppermute(value, axis, pairs)
            step *= 2
        else:
            return lax.psum(value, axis)
    return value


def local(
    mass_per_volume, flow_speed, pressure, cotangent, weight_inner, weight_middle, weight_outer
):
    (state_now, scalars), prepare_pullback = jax.vjp(prepare, mass_per_volume, flow_speed, pressure)
    count = scalars.shape[0]
    first = jnp.concatenate([scalars, cotangent], 0)
    first_x = derive_x(first)
    first_y = derive_y(first)
    first_z = derive_z(first)
    gradients = jnp.stack([first_x[:count], first_y[:count], first_z[:count]])
    spread = jnp.stack([first_x[count:], first_y[count:], first_z[count:]])
    flux_bar = TIME_STEP * spread
    cells = mass_per_volume.shape

    def flux_of(eddy_viscosity):
        return fluxes(mass_per_volume, flow_speed, pressure, gradients, eddy_viscosity)

    _, eddy_pullback = jax.vjp(flux_of, jnp.zeros(cells, jnp.float32))
    (eddy_bar,) = eddy_pullback(flux_bar)
    features = gradients[:, :3].reshape((9, -1))
    eddy, features_bar, inner_bar, middle_bar, outer_bar = network(
        features, eddy_bar.reshape(1, -1), weight_inner, weight_middle, weight_outer
    )
    flux_all, flux_pullback = jax.vjp(
        fluxes, mass_per_volume, flow_speed, pressure, gradients, eddy.reshape(cells)
    )
    pulled = flux_pullback(flux_bar)
    features_bar = features_bar.reshape((3, 3) + cells)
    pulled = (
        pulled[0],
        pulled[1],
        pulled[2],
        pulled[3].at[:, :3].add(features_bar),
        inner_bar,
        middle_bar,
        outer_bar.reshape(-1),
    )
    gradient_bar = pulled[3]
    second_x = derive_x(jnp.concatenate([flux_all[0], gradient_bar[0]], 0))
    second_y = derive_y(jnp.concatenate([flux_all[1], gradient_bar[1]], 0))
    second_z = derive_z(jnp.concatenate([flux_all[2], gradient_bar[2]], 0))
    second = second_x + second_y + second_z
    states = state_now.shape[0]
    state_next = state_now - TIME_STEP * second[:states]
    scalar_bar = -second[states:]
    direct = prepare_pullback((cotangent, scalar_bar))
    weights = (pulled[4], pulled[5], pulled[6])
    flat = jnp.concatenate([w.reshape(-1) for w in weights])
    for axis in ("gz", "gy", "gx"):
        flat = butterfly_sum(flat, axis)
    cells_all = (
        mass_per_volume.size * lax.axis_size("gx") * lax.axis_size("gy") * lax.axis_size("gz")
    )
    factor = 1.0 / math.sqrt(cells_all)
    totals = []
    start = 0
    for w in weights:
        totals.append(flat[start : start + w.size].reshape(w.shape) * factor)
        start += w.size
    return (
        state_next,
        direct[0] + pulled[0],
        direct[1] + pulled[1],
        direct[2] + pulled[2],
        totals[0],
        totals[1],
        totals[2],
    )


def solution(mesh):
    placed = (
        P("gz", "gx", "gy"),
        P(None, "gz", "gx", "gy"),
        P("gz", "gx", "gy"),
        P(None, "gz", "gx", "gy"),
        P(),
        P(),
        P(),
    )
    return jax.shard_map(
        local,
        mesh=mesh,
        in_specs=placed,
        out_specs=(
            P(None, "gz", "gx", "gy"),
            P("gz", "gx", "gy"),
            P(None, "gz", "gx", "gy"),
            P("gz", "gx", "gy"),
            P(),
            P(),
            P(),
        ),
        check_vma=False,
    )
```

profile of v0, /device:TPU:1, one launch (start us, length us, event | category | flops | bytes accessed | tf_op | source)
XLA Modules:
  0.0 135.7 jit_solution(866723243395557012)
XLA Ops:
  0.7 0.9 divide_bitcast_fusion
  1.6 1.5 %convolution_bitcast_fusion.1 = f32[9,8,8,128]{3,2,1,0:T(8,128)S(1)} fusion(f32[8,16,1,1]{1,0,3,2:T(8,128)} %constant.120, f32[5,8,16,128]{3,2,1,0:T(8,128)} %param.16, f32[1,8,16,128]{3,2,1,0:T(8,128)S(1)} %divide_bitcast_fusion, f32[3,8,16,128]{3,2,1,0:T(8,128)} %param.14), kind=kOutput, calls=%fused_computation.17 | convolution fusion | flops 14450688 | bytes 885248 | tf_op jit(solution)/shard_map/pj,fzjy->fzpy/dot_general | solution.py:214
  3.1 0.7 fusion.109
  3.8 3.7 %collective-permute-start = (f32[9,8,1,128]{3,2,1,0:T(1,128)}, f32[9,8,1,128]{3,2,1,0:T(1,128)}, u32[]{:S(2)}, u32[]{:S(2)}) collective-permute-start(f32[9,8,1,128]{3,2,1,0:T(1,128)} %get-tuple-element.111), channel_id=1, source_target_pairs={{0,16},{8,24},{16,32},{24,40},{32,48},{40,56},{48,64},{56,72},{64,... | collective-permute-start | bytes 110600 | tf_op jit(solution)/shard_map/ppermute | solution.py:27
  7.6 5.3 %collective-permute-start.3 = (f32[9,8,1,128]{3,2,1,0:T(1,128)}, f32[9,8,1,128]{3,2,1,0:T(1,128)}, u32[]{:S(2)}, u32[]{:S(2)}) collective-permute-start(f32[9,8,1,128]{3,2,1,0:T(1,128)} %get-tuple-element.112), channel_id=1, source_target_pairs={{0,240},{8,248},{16,0},{24,8},{32,16},{40,24},{48,32},{56,40},{64,... | collective-permute-start | bytes 110600 | tf_op jit(solution)/shard_map/ppermute | solution.py:27
  12.8 0.8 fusion.110
  14.3 1.1 copy.27
  15.4 1.2 collective-permute-start.5
  17.1 1.5 %collective-permute-start.4 = (f32[9,8,16,3]{2,1,3,0:T(8,128)S(1)}, f32[9,8,16,3]{2,1,3,0:T(8,128)S(1)}, u32[]{:S(2)}, u32[]{:S(2)}) collective-permute-start(f32[9,8,16,3]{2,1,3,0:T(8,128)S(1)} %copy.25), channel_id=1, source_target_pairs={{0,6},{2,0},{4,2},{6,4},{1,7},{3,1},{5,3},{7,5},{8,14},{10,8},{12,... | collective-permute-start | bytes 41480 | tf_op jit(solution)/shard_map/ppermute | solution.py:27
  20.1 0.7 copy.31.outer_ref
  20.8 0.7 copy.30.inner_ref
  21.5 0.7 copy.29
  22.2 4.4 %collective-permute-start.2 = (f32[9,8,3,128]{3,2,1,0:T(4,128)}, f32[9,8,3,128]{3,2,1,0:T(4,128)}, u32[]{:S(2)}, u32[]{:S(2)}) collective-permute-start(f32[9,8,3,128]{3,2,1,0:T(4,128)} %get-tuple-element.114), channel_id=1, source_target_pairs={{0,248},{8,0},{16,8},{24,16},{32,24},{40,32},{48,40},{56,48},{64,5... | collective-permute-start | bytes 331784 | tf_op jit(solution)/shard_map/ppermute | solution.py:27
  27.1 2.3 %collective-permute-start.6 = (f32[9,6,16,128]{3,2,1,0:T(8,128)S(1)}, f32[9,6,16,128]{3,2,1,0:T(8,128)S(1)}, u32[]{:S(2)}, u32[]{:S(2)}) collective-permute-start(f32[9,6,16,128]{3,2,1,0:T(8,128)S(1)} %pad_maximum_fusion.9), channel_id=1, source_target_pairs={{0,1},{1,0},{2,3},{3,2},{4,5},{5,4},{6,7},{7,6},{8,9},{9,8},{10,11... | collective-permute-start | bytes 1327112 | tf_op jit(solution)/shard_map/ppermute | solution.py:27
  30.4 0.8 fusion.35
  31.2 1.6 %fusion = f32[9,8,16,128]{3,2,1,0:T(8,128)S(1)} fusion(f32[9,8,128,16]{2,3,1,0:T(8,128)S(1)} %fusion.97, f32[16,8,1,1]{0,1,3,2:T(8,128)S(1)} %copy-done.40, f32[9,8,1,128]{3,2,1,0:T(1,128)} %collective-permute-done.3, f32[9,8,3,128]{3,2,1,0:T(4,128)} %collective-permute-done.2, f32[9,8,3,128]{3,2,1,0:T(4,128)S(1)} %collective-permute-done.1, ...), kind=kOutput, calls=%fused_computation.10 | convolution fusion | flops 14524416 | bytes 1475072 | tf_op jit(solution)/shard_map/ij,fzjy->fziy/dot_general | solution.py:227
  33.6 0.8 copy-done.2
  34.4 0.8 fusion.100
  35.2 0.7 add_bitcast_fusion.2
  36.0 0.7 bitcast_dynamic-update-slice_fusion.4
  36.7 1.1 reshape.131.features_ref
  37.8 22.0 %shard_map.162 = (f32[1,16384]{1,0:T(1,128)}, f32[9,16384]{1,0:T(8,128)}, f32[64,9]{1,0:T(8,128)}, f32[64,64]{1,0:T(8,128)}, f32[64,1]{1,0:T(8,128)}) custom-call(f32[9,16384]{1,0:T(8,128)} %reshape.131.features_ref, f32[1,16384]{1,0:T(1,128)} %bitcast.644, f32[64,9]{1,0:T(8,128)} %copy.30.inner_ref, f32[9,64]{1,0:T(8,128)} %bitcast.648, ...), custom_call_target="tpu_custom_call" | custom-call | tf_op jit(solution)/shard_map/pallas_call | solution.py:131
  59.8 1.4 %copy.40 = f32[2,8,128,128]{3,2,1,0:T(8,128)S(1)} copy(f32[2,8,128,128]{3,1,2,0:T(8,128)} %bitcast.643) | data formatting | bytes 2097152
  61.3 1.5 %reshape.136 = f32[576]{0:T(1024)} reshape(f32[64,9]{1,0:T(8,128)} %get-tuple-element.26) | data formatting | bytes 4608 | tf_op jit(solution)/shard_map/reshape | solution.py:329
  62.8 0.8 reshape.137
  63.6 1.4 %reduce.2 = f32[64]{0:T(128)} reduce(f32[64,1]{1,0:T(8,128)} %get-tuple-element.28, f32[]{:T(128)} %constant.122), dimensions={1}, to_apply=%get-tuple-element.28.reduce_sub_computation | reduce | bytes 516 | tf_op jit(solution)/shard_map/pallas_call | solution.py:131
  65.0 1.4 %concatenate.101 = f32[4736]{0:T(1024)} concatenate(f32[576]{0:T(1024)} %reshape.136, f32[4096]{0:T(1024)S(1)} %reshape.137, f32[64]{0:T(128)} %reduce.2), dimensions={0} | concatenate | bytes 37888 | tf_op jit(solution)/shard_map/concatenate | solution.py:329
  66.8 0.9 bitcast_dynamic-update-slice_fusion.8
  70.3 0.7 collective-permute-start.15
  71.0 0.7 fusion.107
  71.7 5.1 %collective-permute-start.10 = (f32[9,8,1,128]{3,2,1,0:T(1,128)}, f32[9,8,1,128]{3,2,1,0:T(1,128)}, u32[]{:S(2)}, u32[]{:S(2)}) collective-permute-start(f32[9,8,1,128]{3,2,1,0:T(1,128)} %get-tuple-element.108), channel_id=1, source_target_pairs={{0,240},{8,248},{16,0},{24,8},{32,16},{40,24},{48,32},{56,40},{64,... | collective-permute-start | bytes 110600 | tf_op jit(solution)/shard_map/ppermute | solution.py:27
  76.8 2.7 %collective-permute-start.16 = (f32[4736]{0:T(1024)S(1)}, f32[4736]{0:T(1024)S(1)}, u32[]{:S(2)}, u32[]{:S(2)}) collective-permute-start(f32[4736]{0:T(1024)S(1)} %add.154), channel_id=1, source_target_pairs={{0,4},{2,6},{4,0},{6,2},{1,5},{3,7},{5,1},{7,3},{8,12},{10,14},{12... | collective-permute-start | bytes 56840 | tf_op jit(solution)/shard_map/ppermute | solution.py:275
  79.7 1.3 collective-permute-done.16
  81.0 1.0 collective-permute-start.17
  82.0 1.4 %fusion.111 = f32[9,8,128,16]{2,3,1,0:T(8,128)} fusion(f32[9,8,16,128]{3,2,1,0:T(8,128)S(1)} %get-tuple-element.81, f32[16,16,1,1]{1,0,3,2:T(8,128)S(1)} %copy-done.37), kind=kOutput, calls=%fused_computation.285 | convolution fusion | flops 28311552 | bytes 1180672 | tf_op jit(solution)/shard_map/ij,fzjy->fziy/dot_general | solution.py:226
  83.8 0.8 multiply_bitcast_fusion.8
  84.6 3.4 %collective-permute-done.18 = f32[4736]{0:T(1024)S(1)} collective-permute-done((f32[4736]{0:T(1024)S(1)}, f32[4736]{0:T(1024)S(1)}, u32[]{:S(2)}, u32[]{:S(2)}) %collective-permute-start.18) | collective-permute-done | bytes 18976 | tf_op jit(solution)/shard_map/ppermute | solution.py:275
  87.9 0.8 fusion.102
  88.7 2.1 %collective-permute-done.19 = f32[4736]{0:T(1024)S(1)} collective-permute-done((f32[4736]{0:T(1024)S(1)}, f32[4736]{0:T(1024)S(1)}, u32[]{:S(2)}, u32[]{:S(2)}) %collective-permute-start.19) | collective-permute-done | bytes 18976 | tf_op jit(solution)/shard_map/ppermute | solution.py:275
  91.5 1.5 %collective-permute-start.20 = (f32[4736]{0:T(1024)}, f32[4736]{0:T(1024)}, u32[]{:S(2)}, u32[]{:S(2)}) collective-permute-start(f32[4736]{0:T(1024)} %add.158), channel_id=1, source_target_pairs={{0,64},{8,72},{16,80},{24,88},{32,96},{40,104},{48,112},{56,120},{... | collective-permute-start | bytes 56840 | tf_op jit(solution)/shard_map/ppermute | solution.py:275
  93.0 0.8 fusion.108
  93.7 1.1 copy.32
  94.9 1.1 copy.34
  96.0 0.8 collective-permute-start.12
  96.8 1.9 %collective-permute-start.11 = (f32[9,8,16,3]{2,1,3,0:T(8,128)}, f32[9,8,16,3]{2,1,3,0:T(8,128)S(1)}, u32[]{:S(2)}, u32[]{:S(2)}) collective-permute-start(f32[9,8,16,3]{2,1,3,0:T(8,128)} %copy.32), channel_id=1, source_target_pairs={{0,6},{2,0},{4,2},{6,4},{1,7},{3,1},{5,3},{7,5},{8,14},{10,8},{12,... | collective-permute-start | bytes 41480 | tf_op jit(solution)/shard_map/ppermute | solution.py:27
  98.7 1.4 add.159
  100.0 2.6 %collective-permute-start.21 = (f32[4736]{0:T(1024)}, f32[4736]{0:T(1024)}, u32[]{:S(2)}, u32[]{:S(2)}) collective-permute-start(f32[4736]{0:T(1024)} %add.159), channel_id=1, source_target_pairs={{0,128},{8,136},{16,144},{24,152},{32,160},{40,168},{48,176},{56,1... | collective-permute-start | bytes 56840 | tf_op jit(solution)/shard_map/ppermute | solution.py:275
  102.6 1.8 %pad_maximum_fusion.10 = f32[9,6,16,128]{3,2,1,0:T(8,128)} fusion(f32[9,3,16,128]{3,2,1,0:T(8,128)} %get-tuple-element.85, f32[9,3,16,128]{3,2,1,0:T(8,128)} %get-tuple-element.84), kind=kLoop, calls=%fused_computation.80 | loop fusion | flops 110592 | bytes 884736 | tf_op jit(solution)/shard_map/concatenate | solution.py:238
  105.7 1.4 %copy.33 = f32[9,8,16,3]{3,2,1,0:T(8,128)S(1)} copy(f32[9,8,16,3]{2,1,3,0:T(8,128)} %copy-done.33) | data formatting | bytes 27648 | tf_op jit(solution)/shard_map/ppermute | solution.py:27
  107.1 4.3 %collective-permute-start.9 = (f32[9,8,3,128]{3,2,1,0:T(4,128)}, f32[9,8,3,128]{3,2,1,0:T(4,128)}, u32[]{:S(2)}, u32[]{:S(2)}) collective-permute-start(f32[9,8,3,128]{3,2,1,0:T(4,128)} %get-tuple-element.110), channel_id=1, source_target_pairs={{0,248},{8,0},{16,8},{24,16},{32,24},{40,32},{48,40},{56,48},{64,5... | collective-permute-start | bytes 331784 | tf_op jit(solution)/shard_map/ppermute | solution.py:27
  111.4 2.2 %copy.35 = f32[9,8,16,3]{3,2,1,0:T(8,128)} copy(f32[9,8,16,3]{2,1,3,0:T(8,128)} %collective-permute-done.12) | data formatting | bytes 27648 | tf_op jit(solution)/shard_map/ppermute | solution.py:27
  113.6 6.7 %collective-permute-start.13 = (f32[9,6,16,128]{3,2,1,0:T(8,128)}, f32[9,6,16,128]{3,2,1,0:T(8,128)}, u32[]{:S(2)}, u32[]{:S(2)}) collective-permute-start(f32[9,6,16,128]{3,2,1,0:T(8,128)} %pad_maximum_fusion.10), channel_id=1, source_target_pairs={{0,1},{1,0},{2,3},{3,2},{4,5},{5,4},{6,7},{7,6},{8,9},{9,8},{10,11... | collective-permute-start | bytes 1327112 | tf_op jit(solution)/shard_map/ppermute | solution.py:27
  120.2 0.7 add.160
  121.7 0.7 mul.609
  122.4 0.7 slice_multiply_fusion.2
  123.0 0.8 mul.606
  123.8 1.4 %copy.36 = f32[64,9]{0,1:T(8,128)} copy(f32[64,9]{1,0:T(8,128)} %mul.606) | data formatting | bytes 4608
  125.2 1.3 slice_multiply_fusion.3
  126.5 1.1 fusion.105
  127.6 4.6 %fusion.3 = f32[9,8,16,128]{3,2,1,0:T(8,128)S(1)} fusion(f32[9,8,128,16]{2,3,1,0:T(8,128)S(1)} %copy-done.14, f32[16,8,1,1]{0,1,3,2:T(8,128)} %constant.121, f32[9,8,16,128]{3,2,1,0:T(8,128)} %copy-done.20, f32[9,3,16,128]{3,2,1,0:T(8,128)S(1)} %get-tuple-element.95, f32[9,3,16,128]{3,2,1,0:T(8,128)S(1)} %get-tuple-element.94, f32[9,8,16,3]{3,2,1,0:T(8,128)} %copy.35, ...), kind=kOutput, calls=%fused_computation.13 | convolution fusion | flops 18948096 | bytes 3124736 | tf_op jit(solution)/shard_map/ij,fzjy->fziy/dot_general | solution.py:227
  132.3 0.7 fusion.62
  133.3 0.7 fusion.60
  134.2 0.8 fusion.57
  135.0 0.8 fusion.39
  (150 shorter events, 11.2 us)
Async XLA Ops:
  0.6 13.4 %copy-start = (f32[3,8,16,128]{3,2,1,0:T(8,128)S(1)}, f32[3,8,16,128]{3,2,1,0:T(8,128)}, u32[]{:S(2)}) copy-start(f32[3,8,16,128]{3,2,1,0:T(8,128)} %param.14) | copy-start | bytes 589828
  0.6 13.4 %copy-start.1 = (f32[5,8,16,128]{3,2,1,0:T(8,128)S(1)}, f32[5,8,16,128]{3,2,1,0:T(8,128)}, u32[]{:S(2)}) copy-start(f32[5,8,16,128]{3,2,1,0:T(8,128)} %param.16) | copy-start | bytes 983044
  3.8 27.4 %collective-permute-start = (f32[9,8,1,128]{3,2,1,0:T(1,128)}, f32[9,8,1,128]{3,2,1,0:T(1,128)}, u32[]{:S(2)}, u32[]{:S(2)}) collective-permute-start(f32[9,8,1,128]{3,2,1,0:T(1,128)} %get-tuple-element.111), channel_id=1, source_target_pairs={{0,16},{8,24},{16,32},{24,40},{32,48},{40,56},{48,64},{56,72},{64,... | collective-permute-start | bytes 110600 | tf_op jit(solution)/shard_map/ppermute | solution.py:27
  7.6 23.6 %collective-permute-start.3 = (f32[9,8,1,128]{3,2,1,0:T(1,128)}, f32[9,8,1,128]{3,2,1,0:T(1,128)}, u32[]{:S(2)}, u32[]{:S(2)}) collective-permute-start(f32[9,8,1,128]{3,2,1,0:T(1,128)} %get-tuple-element.112), channel_id=1, source_target_pairs={{0,240},{8,248},{16,0},{24,8},{32,16},{40,24},{48,32},{56,40},{64,... | collective-permute-start | bytes 110600 | tf_op jit(solution)/shard_map/ppermute | solution.py:27
  13.6 17.6 %collective-permute-start.1 = (f32[9,8,3,128]{3,2,1,0:T(4,128)}, f32[9,8,3,128]{3,2,1,0:T(4,128)S(1)}, u32[]{:S(2)}, u32[]{:S(2)}) collective-permute-start(f32[9,8,3,128]{3,2,1,0:T(4,128)} %get-tuple-element.113), channel_id=1, source_target_pairs={{0,8},{8,16},{16,24},{24,32},{32,40},{40,48},{48,56},{56,64},{64,7... | collective-permute-start | bytes 331784 | tf_op jit(solution)/shard_map/ppermute | solution.py:27
  15.4 3.9 %copy-start.36 = (f32[16,16,1,1]{1,0,3,2:T(8,128)S(1)}, f32[16,16,1,1]{1,0,3,2:T(8,128)}, u32[]{:S(2)}) copy-start(f32[16,16,1,1]{1,0,3,2:T(8,128)} %constant.119) | copy-start | bytes 3076
  15.4 11.7 %collective-permute-start.5 = (f32[9,8,16,3]{2,1,3,0:T(8,128)}, f32[9,8,16,3]{2,1,3,0:T(8,128)S(1)}, u32[]{:S(2)}, u32[]{:S(2)}) collective-permute-start(f32[9,8,16,3]{2,1,3,0:T(8,128)} %copy.27), channel_id=1, source_target_pairs={{0,2},{2,4},{4,6},{6,0},{1,3},{3,5},{5,7},{7,1},{8,10},{10,12},{12... | collective-permute-start | bytes 41480 | tf_op jit(solution)/shard_map/ppermute | solution.py:27
  17.1 5.1 %collective-permute-start.4 = (f32[9,8,16,3]{2,1,3,0:T(8,128)S(1)}, f32[9,8,16,3]{2,1,3,0:T(8,128)S(1)}, u32[]{:S(2)}, u32[]{:S(2)}) collective-permute-start(f32[9,8,16,3]{2,1,3,0:T(8,128)S(1)} %copy.25), channel_id=1, source_target_pairs={{0,6},{2,0},{4,2},{6,4},{1,7},{3,1},{5,3},{7,5},{8,14},{10,8},{12,... | collective-permute-start | bytes 41480 | tf_op jit(solution)/shard_map/ppermute | solution.py:27
  19.4 0.7 copy-start.41
  19.4 1.4 %copy-start.38 = (f32[64,9]{0,1:T(8,128)S(1)}, f32[64,9]{0,1:T(8,128)}, u32[]{:S(2)}) copy-start(f32[64,9]{0,1:T(8,128)} %param.17) | copy-start | bytes 6916
  19.4 2.1 %copy-start.32 = (f32[64,64]{1,0:T(8,128)S(1)}, f32[64,64]{1,0:T(8,128)}, u32[]{:S(2)}) copy-start(f32[64,64]{1,0:T(8,128)} %middle_ref.1) | copy-start | bytes 49156
  22.2 9.0 %collective-permute-start.2 = (f32[9,8,3,128]{3,2,1,0:T(4,128)}, f32[9,8,3,128]{3,2,1,0:T(4,128)}, u32[]{:S(2)}, u32[]{:S(2)}) collective-permute-start(f32[9,8,3,128]{3,2,1,0:T(4,128)} %get-tuple-element.114), channel_id=1, source_target_pairs={{0,248},{8,0},{16,8},{24,16},{32,24},{40,32},{48,40},{56,48},{64,5... | collective-permute-start | bytes 331784 | tf_op jit(solution)/shard_map/ppermute | solution.py:27
  27.1 5.8 %collective-permute-start.6 = (f32[9,6,16,128]{3,2,1,0:T(8,128)S(1)}, f32[9,6,16,128]{3,2,1,0:T(8,128)S(1)}, u32[]{:S(2)}, u32[]{:S(2)}) collective-permute-start(f32[9,6,16,128]{3,2,1,0:T(8,128)S(1)} %pad_maximum_fusion.9), channel_id=1, source_target_pairs={{0,1},{1,0},{2,3},{3,2},{4,5},{5,4},{6,7},{7,6},{8,9},{9,8},{10,11... | collective-permute-start | bytes 1327112 | tf_op jit(solution)/shard_map/ppermute | solution.py:27
  30.3 0.9 copy-start.40
  33.5 0.8 copy-start.2
  34.4 0.8 copy-start.11
  34.4 0.9 copy-start.17
  36.0 0.7 copy-start.6
  36.0 0.7 copy-start.3
  66.3 1.4 %copy-start.9 = (f32[8,16,128]{2,1,0:T(8,128)S(1)}, f32[8,16,128]{2,1,0:T(8,128)}, u32[]{:S(2)}) copy-start(f32[8,16,128]{2,1,0:T(8,128)} %get-tuple-element.51) | copy-start | bytes 196612
  66.3 1.5 %copy-start.19 = (f32[9,8,16,128]{3,2,1,0:T(8,128)S(1)}, f32[9,8,16,128]{3,2,1,0:T(8,128)}, u32[]{:S(2)}) copy-start(f32[9,8,16,128]{3,2,1,0:T(8,128)} %bitcast_dynamic-update-slice_fusion.4) | copy-start | bytes 1769476
  66.3 3.8 %collective-permute-start.14 = (f32[4736]{0:T(1024)}, f32[4736]{0:T(1024)S(1)}, u32[]{:S(2)}, u32[]{:S(2)}) collective-permute-start(f32[4736]{0:T(1024)} %concatenate.101), channel_id=1, source_target_pairs={{0,1},{1,0},{2,3},{3,2},{4,5},{5,4},{6,7},{7,6},{8,9},{9,8},{10,11... | collective-permute-start | bytes 56840 | tf_op jit(solution)/shard_map/ppermute | solution.py:275
  66.8 1.1 copy-start.4
  66.8 1.1 copy-start.12
  67.7 0.8 copy-start.7
  68.7 0.8 copy-start.15
  68.9 0.8 copy-start.39
  69.6 0.7 copy-start.35
  69.7 18.3 %copy-start.20 = (f32[9,8,16,128]{3,2,1,0:T(8,128)}, f32[9,8,16,128]{3,2,1,0:T(8,128)S(1)}, u32[]{:S(2)}) copy-start(f32[9,8,16,128]{3,2,1,0:T(8,128)S(1)} %get-tuple-element.80) | copy-start | bytes 1769476
  70.3 6.4 %collective-permute-start.15 = (f32[4736]{0:T(1024)S(1)}, f32[4736]{0:T(1024)S(1)}, u32[]{:S(2)}, u32[]{:S(2)}) collective-permute-start(f32[4736]{0:T(1024)S(1)} %add.153), channel_id=1, source_target_pairs={{0,2},{2,0},{4,6},{6,4},{1,3},{3,1},{5,7},{7,5},{8,10},{10,8},{12,... | collective-permute-start | bytes 56840 | tf_op jit(solution)/shard_map/ppermute | solution.py:275
  71.7 55.9 %collective-permute-start.7 = (f32[9,8,1,128]{3,2,1,0:T(1,128)}, f32[9,8,1,128]{3,2,1,0:T(1,128)}, u32[]{:S(2)}, u32[]{:S(2)}) collective-permute-start(f32[9,8,1,128]{3,2,1,0:T(1,128)} %get-tuple-element.107), channel_id=1, source_target_pairs={{0,16},{8,24},{16,32},{24,40},{32,48},{40,56},{48,64},{56,72},{64,... | collective-permute-start | bytes 110600 | tf_op jit(solution)/shard_map/ppermute | solution.py:27
  71.7 55.9 %collective-permute-start.10 = (f32[9,8,1,128]{3,2,1,0:T(1,128)}, f32[9,8,1,128]{3,2,1,0:T(1,128)}, u32[]{:S(2)}, u32[]{:S(2)}) collective-permute-start(f32[9,8,1,128]{3,2,1,0:T(1,128)} %get-tuple-element.108), channel_id=1, source_target_pairs={{0,240},{8,248},{16,0},{24,8},{32,16},{40,24},{48,32},{56,40},{64,... | collective-permute-start | bytes 110600 | tf_op jit(solution)/shard_map/ppermute | solution.py:27
  76.8 4.2 %collective-permute-start.16 = (f32[4736]{0:T(1024)S(1)}, f32[4736]{0:T(1024)S(1)}, u32[]{:S(2)}, u32[]{:S(2)}) collective-permute-start(f32[4736]{0:T(1024)S(1)} %add.154), channel_id=1, source_target_pairs={{0,4},{2,6},{4,0},{6,2},{1,5},{3,7},{5,1},{7,3},{8,12},{10,14},{12... | collective-permute-start | bytes 56840 | tf_op jit(solution)/shard_map/ppermute | solution.py:275
  79.5 2.5 %copy-start.37 = (f32[16,16,1,1]{1,0,3,2:T(8,128)S(1)}, f32[16,16,1,1]{1,0,3,2:T(8,128)}, u32[]{:S(2)}) copy-start(f32[16,16,1,1]{1,0,3,2:T(8,128)} %constant.119) | copy-start | bytes 3076
  81.0 2.6 %collective-permute-start.17 = (f32[4736]{0:T(1024)S(1)}, f32[4736]{0:T(1024)S(1)}, u32[]{:S(2)}, u32[]{:S(2)}) collective-permute-start(f32[4736]{0:T(1024)S(1)} %add.155), channel_id=1, source_target_pairs={{0,8},{8,0},{16,24},{24,16},{32,40},{40,32},{48,56},{56,48},{64,72... | collective-permute-start | bytes 56840 | tf_op jit(solution)/shard_map/ppermute | solution.py:275
  83.6 4.3 %collective-permute-start.18 = (f32[4736]{0:T(1024)S(1)}, f32[4736]{0:T(1024)S(1)}, u32[]{:S(2)}, u32[]{:S(2)}) collective-permute-start(f32[4736]{0:T(1024)S(1)} %add.156), channel_id=1, source_target_pairs={{0,16},{8,24},{16,0},{24,8},{32,48},{40,56},{48,32},{56,40},{64,80... | collective-permute-start | bytes 56840 | tf_op jit(solution)/shard_map/ppermute | solution.py:275
  87.9 2.9 %collective-permute-start.19 = (f32[4736]{0:T(1024)S(1)}, f32[4736]{0:T(1024)S(1)}, u32[]{:S(2)}, u32[]{:S(2)}) collective-permute-start(f32[4736]{0:T(1024)S(1)} %add.157), channel_id=1, source_target_pairs={{0,32},{8,40},{16,48},{24,56},{32,0},{40,8},{48,16},{56,24},{64,96... | collective-permute-start | bytes 56840 | tf_op jit(solution)/shard_map/ppermute | solution.py:275
  91.5 7.2 %collective-permute-start.20 = (f32[4736]{0:T(1024)}, f32[4736]{0:T(1024)}, u32[]{:S(2)}, u32[]{:S(2)}) collective-permute-start(f32[4736]{0:T(1024)} %add.158), channel_id=1, source_target_pairs={{0,64},{8,72},{16,80},{24,88},{32,96},{40,104},{48,112},{56,120},{... | collective-permute-start | bytes 56840 | tf_op jit(solution)/shard_map/ppermute | solution.py:275
  96.0 11.1 %collective-permute-start.12 = (f32[9,8,16,3]{2,1,3,0:T(8,128)}, f32[9,8,16,3]{2,1,3,0:T(8,128)}, u32[]{:S(2)}, u32[]{:S(2)}) collective-permute-start(f32[9,8,16,3]{2,1,3,0:T(8,128)} %copy.34), channel_id=1, source_target_pairs={{0,2},{2,4},{4,6},{6,0},{1,3},{3,5},{5,7},{7,1},{8,10},{10,12},{12... | collective-permute-start | bytes 41480 | tf_op jit(solution)/shard_map/ppermute | solution.py:27
  96.8 7.7 %collective-permute-start.11 = (f32[9,8,16,3]{2,1,3,0:T(8,128)}, f32[9,8,16,3]{2,1,3,0:T(8,128)S(1)}, u32[]{:S(2)}, u32[]{:S(2)}) collective-permute-start(f32[9,8,16,3]{2,1,3,0:T(8,128)} %copy.32), channel_id=1, source_target_pairs={{0,6},{2,0},{4,2},{6,4},{1,7},{3,1},{5,3},{7,5},{8,14},{10,8},{12,... | collective-permute-start | bytes 41480 | tf_op jit(solution)/shard_map/ppermute | solution.py:27
  100.0 13.5 %collective-permute-start.21 = (f32[4736]{0:T(1024)}, f32[4736]{0:T(1024)}, u32[]{:S(2)}, u32[]{:S(2)}) collective-permute-start(f32[4736]{0:T(1024)} %add.159), channel_id=1, source_target_pairs={{0,128},{8,136},{16,144},{24,152},{32,160},{40,168},{48,176},{56,1... | collective-permute-start | bytes 56840 | tf_op jit(solution)/shard_map/ppermute | solution.py:275
  104.5 0.6 copy-start.33
  105.1 22.5 %copy-start.14 = (f32[9,8,128,16]{2,3,1,0:T(8,128)S(1)}, f32[9,8,128,16]{2,3,1,0:T(8,128)}, u32[]{:S(2)}) copy-start(f32[9,8,128,16]{2,3,1,0:T(8,128)} %fusion.111) | copy-start | bytes 1769476
  105.1 22.5 %collective-permute-start.8 = (f32[9,8,3,128]{3,2,1,0:T(4,128)}, f32[9,8,3,128]{3,2,1,0:T(4,128)}, u32[]{:S(2)}, u32[]{:S(2)}) collective-permute-start(f32[9,8,3,128]{3,2,1,0:T(4,128)} %get-tuple-element.109), channel_id=1, source_target_pairs={{0,8},{8,16},{16,24},{24,32},{32,40},{40,48},{48,56},{56,64},{64,7... | collective-permute-start | bytes 331784 | tf_op jit(solution)/shard_map/ppermute | solution.py:27
  107.1 20.5 %collective-permute-start.9 = (f32[9,8,3,128]{3,2,1,0:T(4,128)}, f32[9,8,3,128]{3,2,1,0:T(4,128)}, u32[]{:S(2)}, u32[]{:S(2)}) collective-permute-start(f32[9,8,3,128]{3,2,1,0:T(4,128)} %get-tuple-element.110), channel_id=1, source_target_pairs={{0,248},{8,0},{16,8},{24,16},{32,24},{40,32},{48,40},{56,48},{64,5... | collective-permute-start | bytes 331784 | tf_op jit(solution)/shard_map/ppermute | solution.py:27
  113.6 12.9 %collective-permute-start.13 = (f32[9,6,16,128]{3,2,1,0:T(8,128)}, f32[9,6,16,128]{3,2,1,0:T(8,128)}, u32[]{:S(2)}, u32[]{:S(2)}) collective-permute-start(f32[9,6,16,128]{3,2,1,0:T(8,128)} %pad_maximum_fusion.10), channel_id=1, source_target_pairs={{0,1},{1,0},{2,3},{3,2},{4,5},{5,4},{6,7},{7,6},{8,9},{9,8},{10,11... | collective-permute-start | bytes 1327112 | tf_op jit(solution)/shard_map/ppermute | solution.py:27
  121.0 0.6 copy-start.34
  132.2 0.8 copy-start.5
  132.2 0.9 copy-start.8
  132.2 0.9 copy-start.10
  132.2 0.9 copy-start.16
  132.3 1.0 copy-start.13
  132.3 1.0 copy-start.18
  132.3 1.0 copy-start.22
  132.3 1.0 copy-start.30
  132.3 1.0 copy-start.31
  133.1 0.9 copy-start.21
  133.1 0.9 copy-start.23
  133.2 0.9 copy-start.24
  133.2 1.0 copy-start.25
  133.2 1.0 copy-start.26
  133.2 1.0 copy-start.27
  133.2 1.0 copy-start.28
  134.1 0.9 copy-start.29
where the time goes:
time: 137 us; the launch traced here: 136 us
  starting transfers between devices  47.3 us (35%)
  local copies, waits for them, and re-layouts  29.9 us (22%)
  Pallas kernels  22 us (16%)
  other arithmetic  18.1 us (13%)
  matrix products  10.2 us (7%)
  waiting for transfers between devices  6.96 us (5%)
    ppermute x14, starting transfers between devices, from_behind(): return lax.ppermute(value, axis, pairs)  38.2 us
    pallas_call x1, Pallas kernels, network(): pl.pallas_call(network_kernel, grid=(cells // block,), in_specs=[lanes(in...  22 us
    ppermute x8, starting transfers between devices, butterfly_sum(): value = value + lax.ppermute(value, axis, pairs)  9.09 us
    unnamed x91, local copies, waits for them, and re-layouts  9.02 us
    ppermute x8, waiting for transfers between devices, butterfly_sum(): value = value + lax.ppermute(value, axis, pairs)  6.92 us
    dot_general x2, matrix products, derive_x(): jnp.einsum('ij,fzjy->fziy', take_received, received, precision=HIGHEST_PR...  6.21 us
    ppermute x4, local copies, waits for them, and re-layouts, from_behind(): return lax.ppermute(value, axis, pairs)  4.59 us
    slice x4, local copies, waits for them, and re-layouts, halo(): low_part = lax.slice_in_dim(block, size - width, size, axis=dim)  3.08 us
  transfers between devices with their start and end apart: 22, of which 4 were waited for; matrix products, arithmetic and copies ran while one was open for 24% of the time, Pallas kernels for 0%

commit v1 on v0

--- a/solution.py
+++ b/solution.py
@@ -18,7 +18,7 @@
 HIGHEST_PRECISION = lax.Precision.HIGHEST
 NEAR_HALO = 2
 NETWORK_PRECISION = lax.Precision.HIGH
-NETWORK_BLOCK = 2048
+NETWORK_BLOCK = 4096
 
 
 def from_behind(value, axis, steps):
@@ -83,26 +83,41 @@
     return fluxes(density_in, velocity_in, pressure_in, upstream_cotangent, eddy_viscosity)
 
 
+def split_bf16(value):
+    high = value.astype(jnp.bfloat16)
+    low = (value - high.astype(jnp.float32)).astype(jnp.bfloat16)
+    return high, low
+
+
+def dot3(left, right, dims=(((1,), (0,)), ((), ()))):
+    left_high, left_low = left
+    right_high, right_low = right
+
+    def one(a, b):
+        return lax.dot_general(a, b, dims, preferred_element_type=jnp.float32)
+
+    return one(left_high, right_high) + (one(left_high, right_low) + one(left_low, right_high))
+
+
 def network_kernel(
     features_ref, eddy_bar_ref, inner_ref, inner_t_ref, middle_ref, middle_t_ref, outer_ref,
     eddy_ref, features_bar_ref, inner_bar_ref, middle_bar_ref, outer_bar_ref,
 ):
-    exact = lax.Precision.HIGHEST
-    features = features_ref[...]
-    first = jnp.tanh(jnp.dot(inner_ref[...], features, precision=exact))
-    second = jnp.tanh(jnp.dot(middle_ref[...], first, precision=exact))
+    features = split_bf16(features_ref[...])
+    first = jnp.tanh(dot3(split_bf16(inner_ref[...]), features))
+    first_split = split_bf16(first)
+    second = jnp.tanh(dot3(split_bf16(middle_ref[...]), first_split))
     output = jnp.sum(outer_ref[...] * second, axis=0, keepdims=True)
     soft = jnp.maximum(output, 0.0) + jnp.log1p(jnp.exp(-jnp.abs(output)))
     eddy_ref[...] = EDDY_SCALE * soft
     output_bar = EDDY_SCALE * eddy_bar_ref[...] / (1.0 + jnp.exp(-output))
-    second_pre_bar = outer_ref[...] * output_bar * (1.0 - second * second)
-    first_pre_bar = jnp.dot(middle_t_ref[...], second_pre_bar, precision=exact) * (
-        1.0 - first * first
-    )
-    features_bar_ref[...] = jnp.dot(inner_t_ref[...], first_pre_bar, precision=exact)
+    second_pre_bar = split_bf16(outer_ref[...] * output_bar * (1.0 - second * second))
+    first_pre_bar = dot3(split_bf16(middle_t_ref[...]), second_pre_bar) * (1.0 - first * first)
+    first_pre_bar = split_bf16(first_pre_bar)
+    features_bar_ref[...] = dot3(split_bf16(inner_t_ref[...]), first_pre_bar)
     by_cells = (((1,), (1,)), ((), ()))
-    middle_part = lax.dot_general(second_pre_bar, first, by_cells, precision=exact)
-    inner_part = lax.dot_general(first_pre_bar, features, by_cells, precision=exact)
+    middle_part = dot3(second_pre_bar, first_split, by_cells)
+    inner_part = dot3(first_pre_bar, features, by_cells)
     outer_part = jnp.sum(second * output_bar, axis=1, keepdims=True)
 
     @pl.when(pl.program_id(0) == 0)

time: 137 us -> 129 us (0.942)
  Pallas kernels: 22 us -> 13.7 us
    pallas_call x1, Pallas kernels: 22 us -> 13.7 us  [network(): pl.pallas_call(network_kernel, grid=(cells // block,), in_specs=[lanes(in...]
  transfers between devices with their start and end apart: 22 -> 22, of which waited for: 4 -> 4; matrix products, arithmetic and copies ran while one was open for 24% -> 26% of each run, Pallas kernels for 0% -> 0%
where the time goes in v1:
time: 129 us; the launch traced here: 127 us
  starting transfers between devices  47.2 us (37%)
  local copies, waits for them, and re-layouts  29.9 us (23%)
  other arithmetic  18.1 us (14%)
  Pallas kernels  13.7 us (11%)
  matrix products  10.2 us (8%)
  waiting for transfers between devices  6.98 us (5%)
  between operations  1.31 us (1%)
    ppermute x14, starting transfers between devices, from_behind(): return lax.ppermute(value, axis, pairs)  38.2 us
    pallas_call x1, Pallas kernels, network(): pl.pallas_call(network_kernel, grid=(cells // block,), in_specs=[lanes(in...  13.7 us
    ppermute x8, starting transfers between devices, butterfly_sum(): value = value + lax.ppermute(value, axis, pairs)  9.06 us
    unnamed x91, local copies, waits for them, and re-layouts  9.02 us
    ppermute x8, waiting for transfers between devices, butterfly_sum(): value = value + lax.ppermute(value, axis, pairs)  6.94 us
    dot_general x2, matrix products, derive_x(): jnp.einsum('ij,fzjy->fziy', take_received, received, precision=HIGHEST_PR...  6.21 us
    ppermute x4, local copies, waits for them, and re-layouts, from_behind(): return lax.ppermute(value, axis, pairs)  4.59 us
    slice x4, local copies, waits for them, and re-layouts, halo(): low_part = lax.slice_in_dim(block, size - width, size, axis=dim)  3.08 us
  transfers between devices with their start and end apart: 22, of which 4 were waited for; matrix products, arithmetic and copies ran while one was open for 26% of the time, Pallas kernels for 0%

profile of v1, /device:TPU:1, one launch (start us, length us, event | category | flops | bytes accessed | tf_op | source)
XLA Modules:
  0.0 127.4 jit_solution(8029015684306422336)
XLA Ops:
  0.7 0.9 divide_bitcast_fusion
  1.6 1.5 %convolution_bitcast_fusion.1 = f32[9,8,8,128]{3,2,1,0:T(8,128)S(1)} fusion(f32[8,16,1,1]{1,0,3,2:T(8,128)} %constant.120, f32[5,8,16,128]{3,2,1,0:T(8,128)} %param.16, f32[1,8,16,128]{3,2,1,0:T(8,128)S(1)} %divide_bitcast_fusion, f32[3,8,16,128]{3,2,1,0:T(8,128)} %param.14), kind=kOutput, calls=%fused_computation.17 | convolution fusion | flops 14450688 | bytes 885248 | tf_op jit(solution)/shard_map/pj,fzjy->fzpy/dot_general | solution.py:229
  3.1 0.7 fusion.109
  3.8 3.7 %collective-permute-start = (f32[9,8,1,128]{3,2,1,0:T(1,128)}, f32[9,8,1,128]{3,2,1,0:T(1,128)}, u32[]{:S(2)}, u32[]{:S(2)}) collective-permute-start(f32[9,8,1,128]{3,2,1,0:T(1,128)} %get-tuple-element.111), channel_id=1, source_target_pairs={{0,16},{8,24},{16,32},{24,40},{32,48},{40,56},{48,64},{56,72},{64,... | collective-permute-start | bytes 110600 | tf_op jit(solution)/shard_map/ppermute | solution.py:27
  7.6 5.3 %collective-permute-start.3 = (f32[9,8,1,128]{3,2,1,0:T(1,128)}, f32[9,8,1,128]{3,2,1,0:T(1,128)}, u32[]{:S(2)}, u32[]{:S(2)}) collective-permute-start(f32[9,8,1,128]{3,2,1,0:T(1,128)} %get-tuple-element.112), channel_id=1, source_target_pairs={{0,240},{8,248},{16,0},{24,8},{32,16},{40,24},{48,32},{56,40},{64,... | collective-permute-start | bytes 110600 | tf_op jit(solution)/shard_map/ppermute | solution.py:27
  12.8 0.8 fusion.110
  14.3 1.1 copy.27
  15.4 1.2 collective-permute-start.5
  17.1 1.5 %collective-permute-start.4 = (f32[9,8,16,3]{2,1,3,0:T(8,128)S(1)}, f32[9,8,16,3]{2,1,3,0:T(8,128)S(1)}, u32[]{:S(2)}, u32[]{:S(2)}) collective-permute-start(f32[9,8,16,3]{2,1,3,0:T(8,128)S(1)} %copy.25), channel_id=1, source_target_pairs={{0,6},{2,0},{4,2},{6,4},{1,7},{3,1},{5,3},{7,5},{8,14},{10,8},{12,... | collective-permute-start | bytes 41480 | tf_op jit(solution)/shard_map/ppermute | solution.py:27
  18.7 0.7 multiply_reduce_fusion
  20.1 0.7 copy.31.outer_ref
  20.8 0.7 copy.30.inner_ref
  21.5 0.7 copy.29
  22.2 4.4 %collective-permute-start.2 = (f32[9,8,3,128]{3,2,1,0:T(4,128)}, f32[9,8,3,128]{3,2,1,0:T(4,128)}, u32[]{:S(2)}, u32[]{:S(2)}) collective-permute-start(f32[9,8,3,128]{3,2,1,0:T(4,128)} %get-tuple-element.114), channel_id=1, source_target_pairs={{0,248},{8,0},{16,8},{24,16},{32,24},{40,32},{48,40},{56,48},{64,5... | collective-permute-start | bytes 331784 | tf_op jit(solution)/shard_map/ppermute | solution.py:27
  27.1 2.3 %collective-permute-start.6 = (f32[9,6,16,128]{3,2,1,0:T(8,128)S(1)}, f32[9,6,16,128]{3,2,1,0:T(8,128)S(1)}, u32[]{:S(2)}, u32[]{:S(2)}) collective-permute-start(f32[9,6,16,128]{3,2,1,0:T(8,128)S(1)} %pad_maximum_fusion.9), channel_id=1, source_target_pairs={{0,1},{1,0},{2,3},{3,2},{4,5},{5,4},{6,7},{7,6},{8,9},{9,8},{10,11... | collective-permute-start | bytes 1327112 | tf_op jit(solution)/shard_map/ppermute | solution.py:27
  30.4 0.8 fusion.35
  31.2 1.6 %fusion = f32[9,8,16,128]{3,2,1,0:T(8,128)S(1)} fusion(f32[9,8,128,16]{2,3,1,0:T(8,128)S(1)} %fusion.97, f32[16,8,1,1]{0,1,3,2:T(8,128)S(1)} %copy-done.40, f32[9,8,1,128]{3,2,1,0:T(1,128)} %collective-permute-done.3, f32[9,8,3,128]{3,2,1,0:T(4,128)} %collective-permute-done.2, f32[9,8,3,128]{3,2,1,0:T(4,128)S(1)} %collective-permute-done.1, ...), kind=kOutput, calls=%fused_computation.10 | convolution fusion | flops 14524416 | bytes 1475072 | tf_op jit(solution)/shard_map/ij,fzjy->fziy/dot_general | solution.py:242
  33.6 0.8 copy-done.2
  34.4 0.8 fusion.100
  35.2 0.7 add_bitcast_fusion.2
  36.0 0.7 bitcast_dynamic-update-slice_fusion.4
  36.7 1.1 reshape.131.features_ref
  37.8 13.7 %shard_map.162 = (f32[1,16384]{1,0:T(1,128)}, f32[9,16384]{1,0:T(8,128)}, f32[64,9]{1,0:T(8,128)}, f32[64,64]{1,0:T(8,128)}, f32[64,1]{1,0:T(8,128)}) custom-call(f32[9,16384]{1,0:T(8,128)} %reshape.131.features_ref, f32[1,16384]{1,0:T(1,128)} %bitcast.644, f32[64,9]{1,0:T(8,128)} %copy.30.inner_ref, f32[9,64]{1,0:T(8,128)} %bitcast.648, ...), custom_call_target="tpu_custom_call" | custom-call | tf_op jit(solution)/shard_map/pallas_call | solution.py:146
  51.5 1.4 %copy.40 = f32[2,8,128,128]{3,2,1,0:T(8,128)S(1)} copy(f32[2,8,128,128]{3,1,2,0:T(8,128)} %bitcast.643) | data formatting | bytes 2097152
  52.9 1.5 %reshape.136 = f32[576]{0:T(1024)} reshape(f32[64,9]{1,0:T(8,128)} %get-tuple-element.26) | data formatting | bytes 4608 | tf_op jit(solution)/shard_map/reshape | solution.py:344
  54.4 0.8 reshape.137
  55.3 1.4 %reduce.2 = f32[64]{0:T(128)} reduce(f32[64,1]{1,0:T(8,128)} %get-tuple-element.28, f32[]{:T(128)} %constant.122), dimensions={1}, to_apply=%get-tuple-element.28.reduce_sub_computation | reduce | bytes 516 | tf_op jit(solution)/shard_map/pallas_call | solution.py:146
  56.6 1.4 %concatenate.101 = f32[4736]{0:T(1024)} concatenate(f32[576]{0:T(1024)} %reshape.136, f32[4096]{0:T(1024)S(1)} %reshape.137, f32[64]{0:T(128)} %reduce.2), dimensions={0} | concatenate | bytes 37888 | tf_op jit(solution)/shard_map/concatenate | solution.py:344
  58.5 0.9 bitcast_dynamic-update-slice_fusion.8
  62.7 0.7 fusion.107
  63.4 5.1 %collective-permute-start.10 = (f32[9,8,1,128]{3,2,1,0:T(1,128)}, f32[9,8,1,128]{3,2,1,0:T(1,128)}, u32[]{:S(2)}, u32[]{:S(2)}) collective-permute-start(f32[9,8,1,128]{3,2,1,0:T(1,128)} %get-tuple-element.108), channel_id=1, source_target_pairs={{0,240},{8,248},{16,0},{24,8},{32,16},{40,24},{48,32},{56,40},{64,... | collective-permute-start | bytes 110600 | tf_op jit(solution)/shard_map/ppermute | solution.py:27
  68.4 2.7 %collective-permute-start.16 = (f32[4736]{0:T(1024)S(1)}, f32[4736]{0:T(1024)S(1)}, u32[]{:S(2)}, u32[]{:S(2)}) collective-permute-start(f32[4736]{0:T(1024)S(1)} %add.154), channel_id=1, source_target_pairs={{0,4},{2,6},{4,0},{6,2},{1,5},{3,7},{5,1},{7,3},{8,12},{10,14},{12... | collective-permute-start | bytes 56840 | tf_op jit(solution)/shard_map/ppermute | solution.py:290
  71.4 1.3 collective-permute-done.16
  72.7 1.0 collective-permute-start.17
  73.7 1.4 %fusion.111 = f32[9,8,128,16]{2,3,1,0:T(8,128)} fusion(f32[9,8,16,128]{3,2,1,0:T(8,128)S(1)} %get-tuple-element.81, f32[16,16,1,1]{1,0,3,2:T(8,128)S(1)} %copy-done.37), kind=kOutput, calls=%fused_computation.285 | convolution fusion | flops 28311552 | bytes 1180672 | tf_op jit(solution)/shard_map/ij,fzjy->fziy/dot_general | solution.py:241
  75.5 0.8 multiply_bitcast_fusion.8
  76.2 3.4 %collective-permute-done.18 = f32[4736]{0:T(1024)S(1)} collective-permute-done((f32[4736]{0:T(1024)S(1)}, f32[4736]{0:T(1024)S(1)}, u32[]{:S(2)}, u32[]{:S(2)}) %collective-permute-start.18) | collective-permute-done | bytes 18976 | tf_op jit(solution)/shard_map/ppermute | solution.py:290
  79.6 0.8 fusion.102
  80.4 2.1 %collective-permute-done.19 = f32[4736]{0:T(1024)S(1)} collective-permute-done((f32[4736]{0:T(1024)S(1)}, f32[4736]{0:T(1024)S(1)}, u32[]{:S(2)}, u32[]{:S(2)}) %collective-permute-start.19) | collective-permute-done | bytes 18976 | tf_op jit(solution)/shard_map/ppermute | solution.py:290
  83.1 1.5 %collective-permute-start.20 = (f32[4736]{0:T(1024)}, f32[4736]{0:T(1024)}, u32[]{:S(2)}, u32[]{:S(2)}) collective-permute-start(f32[4736]{0:T(1024)} %add.158), channel_id=1, source_target_pairs={{0,64},{8,72},{16,80},{24,88},{32,96},{40,104},{48,112},{56,120},{... | collective-permute-start | bytes 56840 | tf_op jit(solution)/shard_map/ppermute | solution.py:290
  84.6 0.8 fusion.108
  85.4 1.1 copy.32
  86.5 1.1 copy.34
  87.6 0.8 collective-permute-start.12
  88.5 1.9 %collective-permute-start.11 = (f32[9,8,16,3]{2,1,3,0:T(8,128)}, f32[9,8,16,3]{2,1,3,0:T(8,128)S(1)}, u32[]{:S(2)}, u32[]{:S(2)}) collective-permute-start(f32[9,8,16,3]{2,1,3,0:T(8,128)} %copy.32), channel_id=1, source_target_pairs={{0,6},{2,0},{4,2},{6,4},{1,7},{3,1},{5,3},{7,5},{8,14},{10,8},{12,... | collective-permute-start | bytes 41480 | tf_op jit(solution)/shard_map/ppermute | solution.py:27
  90.3 1.4 %add.159 = f32[4736]{0:T(1024)} add(f32[4736]{0:T(1024)} %add.158, f32[4736]{0:T(1024)} %collective-permute-done.20) | non-fusion elementwise | flops 4736 | bytes 56832 | tf_op jit(solution)/shard_map/add | solution.py:290
  91.7 2.6 %collective-permute-start.21 = (f32[4736]{0:T(1024)}, f32[4736]{0:T(1024)}, u32[]{:S(2)}, u32[]{:S(2)}) collective-permute-start(f32[4736]{0:T(1024)} %add.159), channel_id=1, source_target_pairs={{0,128},{8,136},{16,144},{24,152},{32,160},{40,168},{48,176},{56,1... | collective-permute-start | bytes 56840 | tf_op jit(solution)/shard_map/ppermute | solution.py:290
  94.3 1.8 %pad_maximum_fusion.10 = f32[9,6,16,128]{3,2,1,0:T(8,128)} fusion(f32[9,3,16,128]{3,2,1,0:T(8,128)} %get-tuple-element.85, f32[9,3,16,128]{3,2,1,0:T(8,128)} %get-tuple-element.84), kind=kLoop, calls=%fused_computation.80 | loop fusion | flops 110592 | bytes 884736 | tf_op jit(solution)/shard_map/concatenate | solution.py:253
  97.4 1.4 %copy.33 = f32[9,8,16,3]{3,2,1,0:T(8,128)S(1)} copy(f32[9,8,16,3]{2,1,3,0:T(8,128)} %copy-done.33) | data formatting | bytes 27648 | tf_op jit(solution)/shard_map/ppermute | solution.py:27
  98.7 4.3 %collective-permute-start.9 = (f32[9,8,3,128]{3,2,1,0:T(4,128)}, f32[9,8,3,128]{3,2,1,0:T(4,128)}, u32[]{:S(2)}, u32[]{:S(2)}) collective-permute-start(f32[9,8,3,128]{3,2,1,0:T(4,128)} %get-tuple-element.110), channel_id=1, source_target_pairs={{0,248},{8,0},{16,8},{24,16},{32,24},{40,32},{48,40},{56,48},{64,5... | collective-permute-start | bytes 331784 | tf_op jit(solution)/shard_map/ppermute | solution.py:27
  103.0 2.2 %copy.35 = f32[9,8,16,3]{3,2,1,0:T(8,128)} copy(f32[9,8,16,3]{2,1,3,0:T(8,128)} %collective-permute-done.12) | data formatting | bytes 27648 | tf_op jit(solution)/shard_map/ppermute | solution.py:27
  105.2 6.7 %collective-permute-start.13 = (f32[9,6,16,128]{3,2,1,0:T(8,128)}, f32[9,6,16,128]{3,2,1,0:T(8,128)}, u32[]{:S(2)}, u32[]{:S(2)}) collective-permute-start(f32[9,6,16,128]{3,2,1,0:T(8,128)} %pad_maximum_fusion.10), channel_id=1, source_target_pairs={{0,1},{1,0},{2,3},{3,2},{4,5},{5,4},{6,7},{7,6},{8,9},{9,8},{10,11... | collective-permute-start | bytes 1327112 | tf_op jit(solution)/shard_map/ppermute | solution.py:27
  111.9 0.7 add.160
  113.3 0.7 mul.609
  114.0 0.7 slice_multiply_fusion.2
  114.7 0.8 mul.606
  115.4 1.4 %copy.36 = f32[64,9]{0,1:T(8,128)} copy(f32[64,9]{1,0:T(8,128)} %mul.606) | data formatting | bytes 4608
  116.9 1.3 slice_multiply_fusion.3
  118.1 1.1 fusion.105
  119.3 4.6 %fusion.3 = f32[9,8,16,128]{3,2,1,0:T(8,128)S(1)} fusion(f32[9,8,128,16]{2,3,1,0:T(8,128)S(1)} %copy-done.14, f32[16,8,1,1]{0,1,3,2:T(8,128)} %constant.121, f32[9,8,16,128]{3,2,1,0:T(8,128)} %copy-done.20, f32[9,3,16,128]{3,2,1,0:T(8,128)S(1)} %get-tuple-element.95, f32[9,3,16,128]{3,2,1,0:T(8,128)S(1)} %get-tuple-element.94, f32[9,8,16,3]{3,2,1,0:T(8,128)} %copy.35, ...), kind=kOutput, calls=%fused_computation.13 | convolution fusion | flops 18948096 | bytes 3124736 | tf_op jit(solution)/shard_map/ij,fzjy->fziy/dot_general | solution.py:242
  124.0 0.7 fusion.62
  125.0 0.7 fusion.60
  125.8 0.8 fusion.57
  126.6 0.8 fusion.39
  (150 shorter events, 11.2 us)
Async XLA Ops:
  0.6 13.4 %copy-start = (f32[3,8,16,128]{3,2,1,0:T(8,128)S(1)}, f32[3,8,16,128]{3,2,1,0:T(8,128)}, u32[]{:S(2)}) copy-start(f32[3,8,16,128]{3,2,1,0:T(8,128)} %param.14) | copy-start | bytes 589828
  0.6 13.4 %copy-start.1 = (f32[5,8,16,128]{3,2,1,0:T(8,128)S(1)}, f32[5,8,16,128]{3,2,1,0:T(8,128)}, u32[]{:S(2)}) copy-start(f32[5,8,16,128]{3,2,1,0:T(8,128)} %param.16) | copy-start | bytes 983044
  3.8 27.4 %collective-permute-start = (f32[9,8,1,128]{3,2,1,0:T(1,128)}, f32[9,8,1,128]{3,2,1,0:T(1,128)}, u32[]{:S(2)}, u32[]{:S(2)}) collective-permute-start(f32[9,8,1,128]{3,2,1,0:T(1,128)} %get-tuple-element.111), channel_id=1, source_target_pairs={{0,16},{8,24},{16,32},{24,40},{32,48},{40,56},{48,64},{56,72},{64,... | collective-permute-start | bytes 110600 | tf_op jit(solution)/shard_map/ppermute | solution.py:27
  7.6 23.6 %collective-permute-start.3 = (f32[9,8,1,128]{3,2,1,0:T(1,128)}, f32[9,8,1,128]{3,2,1,0:T(1,128)}, u32[]{:S(2)}, u32[]{:S(2)}) collective-permute-start(f32[9,8,1,128]{3,2,1,0:T(1,128)} %get-tuple-element.112), channel_id=1, source_target_pairs={{0,240},{8,248},{16,0},{24,8},{32,16},{40,24},{48,32},{56,40},{64,... | collective-permute-start | bytes 110600 | tf_op jit(solution)/shard_map/ppermute | solution.py:27
  13.6 17.6 %collective-permute-start.1 = (f32[9,8,3,128]{3,2,1,0:T(4,128)}, f32[9,8,3,128]{3,2,1,0:T(4,128)S(1)}, u32[]{:S(2)}, u32[]{:S(2)}) collective-permute-start(f32[9,8,3,128]{3,2,1,0:T(4,128)} %get-tuple-element.113), channel_id=1, source_target_pairs={{0,8},{8,16},{16,24},{24,32},{32,40},{40,48},{48,56},{56,64},{64,7... | collective-permute-start | bytes 331784 | tf_op jit(solution)/shard_map/ppermute | solution.py:27
  15.4 3.9 %copy-start.36 = (f32[16,16,1,1]{1,0,3,2:T(8,128)S(1)}, f32[16,16,1,1]{1,0,3,2:T(8,128)}, u32[]{:S(2)}) copy-start(f32[16,16,1,1]{1,0,3,2:T(8,128)} %constant.119) | copy-start | bytes 3076
  15.4 11.7 %collective-permute-start.5 = (f32[9,8,16,3]{2,1,3,0:T(8,128)}, f32[9,8,16,3]{2,1,3,0:T(8,128)S(1)}, u32[]{:S(2)}, u32[]{:S(2)}) collective-permute-start(f32[9,8,16,3]{2,1,3,0:T(8,128)} %copy.27), channel_id=1, source_target_pairs={{0,2},{2,4},{4,6},{6,0},{1,3},{3,5},{5,7},{7,1},{8,10},{10,12},{12... | collective-permute-start | bytes 41480 | tf_op jit(solution)/shard_map/ppermute | solution.py:27
  17.1 5.1 %collective-permute-start.4 = (f32[9,8,16,3]{2,1,3,0:T(8,128)S(1)}, f32[9,8,16,3]{2,1,3,0:T(8,128)S(1)}, u32[]{:S(2)}, u32[]{:S(2)}) collective-permute-start(f32[9,8,16,3]{2,1,3,0:T(8,128)S(1)} %copy.25), channel_id=1, source_target_pairs={{0,6},{2,0},{4,2},{6,4},{1,7},{3,1},{5,3},{7,5},{8,14},{10,8},{12,... | collective-permute-start | bytes 41480 | tf_op jit(solution)/shard_map/ppermute | solution.py:27
  19.4 0.7 copy-start.41
  19.4 1.4 %copy-start.38 = (f32[64,9]{0,1:T(8,128)S(1)}, f32[64,9]{0,1:T(8,128)}, u32[]{:S(2)}) copy-start(f32[64,9]{0,1:T(8,128)} %param.17) | copy-start | bytes 6916
  19.4 2.1 %copy-start.32 = (f32[64,64]{1,0:T(8,128)S(1)}, f32[64,64]{1,0:T(8,128)}, u32[]{:S(2)}) copy-start(f32[64,64]{1,0:T(8,128)} %middle_ref.1) | copy-start | bytes 49156
  22.2 9.0 %collective-permute-start.2 = (f32[9,8,3,128]{3,2,1,0:T(4,128)}, f32[9,8,3,128]{3,2,1,0:T(4,128)}, u32[]{:S(2)}, u32[]{:S(2)}) collective-permute-start(f32[9,8,3,128]{3,2,1,0:T(4,128)} %get-tuple-element.114), channel_id=1, source_target_pairs={{0,248},{8,0},{16,8},{24,16},{32,24},{40,32},{48,40},{56,48},{64,5... | collective-permute-start | bytes 331784 | tf_op jit(solution)/shard_map/ppermute | solution.py:27
  27.1 5.8 %collective-permute-start.6 = (f32[9,6,16,128]{3,2,1,0:T(8,128)S(1)}, f32[9,6,16,128]{3,2,1,0:T(8,128)S(1)}, u32[]{:S(2)}, u32[]{:S(2)}) collective-permute-start(f32[9,6,16,128]{3,2,1,0:T(8,128)S(1)} %pad_maximum_fusion.9), channel_id=1, source_target_pairs={{0,1},{1,0},{2,3},{3,2},{4,5},{5,4},{6,7},{7,6},{8,9},{9,8},{10,11... | collective-permute-start | bytes 1327112 | tf_op jit(solution)/shard_map/ppermute | solution.py:27
  30.3 0.9 copy-start.40
  33.5 0.8 copy-start.2
  34.4 0.8 copy-start.11
  34.4 0.9 copy-start.17
  36.0 0.7 copy-start.6
  36.0 0.7 copy-start.3
  58.0 1.5 %copy-start.9 = (f32[8,16,128]{2,1,0:T(8,128)S(1)}, f32[8,16,128]{2,1,0:T(8,128)}, u32[]{:S(2)}) copy-start(f32[8,16,128]{2,1,0:T(8,128)} %get-tuple-element.51) | copy-start | bytes 196612
  58.0 1.5 %copy-start.19 = (f32[9,8,16,128]{3,2,1,0:T(8,128)S(1)}, f32[9,8,16,128]{3,2,1,0:T(8,128)}, u32[]{:S(2)}) copy-start(f32[9,8,16,128]{3,2,1,0:T(8,128)} %bitcast_dynamic-update-slice_fusion.4) | copy-start | bytes 1769476
  58.0 3.8 %collective-permute-start.14 = (f32[4736]{0:T(1024)}, f32[4736]{0:T(1024)S(1)}, u32[]{:S(2)}, u32[]{:S(2)}) collective-permute-start(f32[4736]{0:T(1024)} %concatenate.101), channel_id=1, source_target_pairs={{0,1},{1,0},{2,3},{3,2},{4,5},{5,4},{6,7},{7,6},{8,9},{9,8},{10,11... | collective-permute-start | bytes 56840 | tf_op jit(solution)/shard_map/ppermute | solution.py:290
  58.5 1.1 copy-start.4
  58.5 1.1 copy-start.12
  59.4 0.8 copy-start.7
  60.4 0.8 copy-start.15
  60.6 0.8 copy-start.39
  61.3 0.7 copy-start.35
  61.3 18.2 %copy-start.20 = (f32[9,8,16,128]{3,2,1,0:T(8,128)}, f32[9,8,16,128]{3,2,1,0:T(8,128)S(1)}, u32[]{:S(2)}) copy-start(f32[9,8,16,128]{3,2,1,0:T(8,128)S(1)} %get-tuple-element.80) | copy-start | bytes 1769476
  62.0 6.4 %collective-permute-start.15 = (f32[4736]{0:T(1024)S(1)}, f32[4736]{0:T(1024)S(1)}, u32[]{:S(2)}, u32[]{:S(2)}) collective-permute-start(f32[4736]{0:T(1024)S(1)} %add.153), channel_id=1, source_target_pairs={{0,2},{2,0},{4,6},{6,4},{1,3},{3,1},{5,7},{7,5},{8,10},{10,8},{12,... | collective-permute-start | bytes 56840 | tf_op jit(solution)/shard_map/ppermute | solution.py:290
  63.4 55.9 %collective-permute-start.7 = (f32[9,8,1,128]{3,2,1,0:T(1,128)}, f32[9,8,1,128]{3,2,1,0:T(1,128)}, u32[]{:S(2)}, u32[]{:S(2)}) collective-permute-start(f32[9,8,1,128]{3,2,1,0:T(1,128)} %get-tuple-element.107), channel_id=1, source_target_pairs={{0,16},{8,24},{16,32},{24,40},{32,48},{40,56},{48,64},{56,72},{64,... | collective-permute-start | bytes 110600 | tf_op jit(solution)/shard_map/ppermute | solution.py:27
  63.4 55.9 %collective-permute-start.10 = (f32[9,8,1,128]{3,2,1,0:T(1,128)}, f32[9,8,1,128]{3,2,1,0:T(1,128)}, u32[]{:S(2)}, u32[]{:S(2)}) collective-permute-start(f32[9,8,1,128]{3,2,1,0:T(1,128)} %get-tuple-element.108), channel_id=1, source_target_pairs={{0,240},{8,248},{16,0},{24,8},{32,16},{40,24},{48,32},{56,40},{64,... | collective-permute-start | bytes 110600 | tf_op jit(solution)/shard_map/ppermute | solution.py:27
  68.4 4.2 %collective-permute-start.16 = (f32[4736]{0:T(1024)S(1)}, f32[4736]{0:T(1024)S(1)}, u32[]{:S(2)}, u32[]{:S(2)}) collective-permute-start(f32[4736]{0:T(1024)S(1)} %add.154), channel_id=1, source_target_pairs={{0,4},{2,6},{4,0},{6,2},{1,5},{3,7},{5,1},{7,3},{8,12},{10,14},{12... | collective-permute-start | bytes 56840 | tf_op jit(solution)/shard_map/ppermute | solution.py:290
  71.2 2.5 %copy-start.37 = (f32[16,16,1,1]{1,0,3,2:T(8,128)S(1)}, f32[16,16,1,1]{1,0,3,2:T(8,128)}, u32[]{:S(2)}) copy-start(f32[16,16,1,1]{1,0,3,2:T(8,128)} %constant.119) | copy-start | bytes 3076
  72.7 2.6 %collective-permute-start.17 = (f32[4736]{0:T(1024)S(1)}, f32[4736]{0:T(1024)S(1)}, u32[]{:S(2)}, u32[]{:S(2)}) collective-permute-start(f32[4736]{0:T(1024)S(1)} %add.155), channel_id=1, source_target_pairs={{0,8},{8,0},{16,24},{24,16},{32,40},{40,32},{48,56},{56,48},{64,72... | collective-permute-start | bytes 56840 | tf_op jit(solution)/shard_map/ppermute | solution.py:290
  75.3 4.3 %collective-permute-start.18 = (f32[4736]{0:T(1024)S(1)}, f32[4736]{0:T(1024)S(1)}, u32[]{:S(2)}, u32[]{:S(2)}) collective-permute-start(f32[4736]{0:T(1024)S(1)} %add.156), channel_id=1, source_target_pairs={{0,16},{8,24},{16,0},{24,8},{32,48},{40,56},{48,32},{56,40},{64,80... | collective-permute-start | bytes 56840 | tf_op jit(solution)/shard_map/ppermute | solution.py:290
  79.6 2.9 %collective-permute-start.19 = (f32[4736]{0:T(1024)S(1)}, f32[4736]{0:T(1024)S(1)}, u32[]{:S(2)}, u32[]{:S(2)}) collective-permute-start(f32[4736]{0:T(1024)S(1)} %add.157), channel_id=1, source_target_pairs={{0,32},{8,40},{16,48},{24,56},{32,0},{40,8},{48,16},{56,24},{64,96... | collective-permute-start | bytes 56840 | tf_op jit(solution)/shard_map/ppermute | solution.py:290
  83.1 7.2 %collective-permute-start.20 = (f32[4736]{0:T(1024)}, f32[4736]{0:T(1024)}, u32[]{:S(2)}, u32[]{:S(2)}) collective-permute-start(f32[4736]{0:T(1024)} %add.158), channel_id=1, source_target_pairs={{0,64},{8,72},{16,80},{24,88},{32,96},{40,104},{48,112},{56,120},{... | collective-permute-start | bytes 56840 | tf_op jit(solution)/shard_map/ppermute | solution.py:290
  87.6 11.1 %collective-permute-start.12 = (f32[9,8,16,3]{2,1,3,0:T(8,128)}, f32[9,8,16,3]{2,1,3,0:T(8,128)}, u32[]{:S(2)}, u32[]{:S(2)}) collective-permute-start(f32[9,8,16,3]{2,1,3,0:T(8,128)} %copy.34), channel_id=1, source_target_pairs={{0,2},{2,4},{4,6},{6,0},{1,3},{3,5},{5,7},{7,1},{8,10},{10,12},{12... | collective-permute-start | bytes 41480 | tf_op jit(solution)/shard_map/ppermute | solution.py:27
  88.5 7.6 %collective-permute-start.11 = (f32[9,8,16,3]{2,1,3,0:T(8,128)}, f32[9,8,16,3]{2,1,3,0:T(8,128)S(1)}, u32[]{:S(2)}, u32[]{:S(2)}) collective-permute-start(f32[9,8,16,3]{2,1,3,0:T(8,128)} %copy.32), channel_id=1, source_target_pairs={{0,6},{2,0},{4,2},{6,4},{1,7},{3,1},{5,3},{7,5},{8,14},{10,8},{12,... | collective-permute-start | bytes 41480 | tf_op jit(solution)/shard_map/ppermute | solution.py:27
  91.7 13.5 %collective-permute-start.21 = (f32[4736]{0:T(1024)}, f32[4736]{0:T(1024)}, u32[]{:S(2)}, u32[]{:S(2)}) collective-permute-start(f32[4736]{0:T(1024)} %add.159), channel_id=1, source_target_pairs={{0,128},{8,136},{16,144},{24,152},{32,160},{40,168},{48,176},{56,1... | collective-permute-start | bytes 56840 | tf_op jit(solution)/shard_map/ppermute | solution.py:290
  96.1 0.6 copy-start.33
  96.8 22.5 %copy-start.14 = (f32[9,8,128,16]{2,3,1,0:T(8,128)S(1)}, f32[9,8,128,16]{2,3,1,0:T(8,128)}, u32[]{:S(2)}) copy-start(f32[9,8,128,16]{2,3,1,0:T(8,128)} %fusion.111) | copy-start | bytes 1769476
  96.8 22.5 %collective-permute-start.8 = (f32[9,8,3,128]{3,2,1,0:T(4,128)}, f32[9,8,3,128]{3,2,1,0:T(4,128)}, u32[]{:S(2)}, u32[]{:S(2)}) collective-permute-start(f32[9,8,3,128]{3,2,1,0:T(4,128)} %get-tuple-element.109), channel_id=1, source_target_pairs={{0,8},{8,16},{16,24},{24,32},{32,40},{40,48},{48,56},{56,64},{64,7... | collective-permute-start | bytes 331784 | tf_op jit(solution)/shard_map/ppermute | solution.py:27
  98.7 20.5 %collective-permute-start.9 = (f32[9,8,3,128]{3,2,1,0:T(4,128)}, f32[9,8,3,128]{3,2,1,0:T(4,128)}, u32[]{:S(2)}, u32[]{:S(2)}) collective-permute-start(f32[9,8,3,128]{3,2,1,0:T(4,128)} %get-tuple-element.110), channel_id=1, source_target_pairs={{0,248},{8,0},{16,8},{24,16},{32,24},{40,32},{48,40},{56,48},{64,5... | collective-permute-start | bytes 331784 | tf_op jit(solution)/shard_map/ppermute | solution.py:27
  105.2 12.9 %collective-permute-start.13 = (f32[9,6,16,128]{3,2,1,0:T(8,128)}, f32[9,6,16,128]{3,2,1,0:T(8,128)}, u32[]{:S(2)}, u32[]{:S(2)}) collective-permute-start(f32[9,6,16,128]{3,2,1,0:T(8,128)} %pad_maximum_fusion.10), channel_id=1, source_target_pairs={{0,1},{1,0},{2,3},{3,2},{4,5},{5,4},{6,7},{7,6},{8,9},{9,8},{10,11... | collective-permute-start | bytes 1327112 | tf_op jit(solution)/shard_map/ppermute | solution.py:27
  112.6 0.6 copy-start.34
  123.9 0.8 copy-start.5
  123.9 0.9 copy-start.8
  123.9 0.9 copy-start.10
  123.9 0.9 copy-start.16
  123.9 1.0 copy-start.13
  123.9 1.0 copy-start.18
  123.9 1.0 copy-start.22
  124.0 1.0 copy-start.30
  124.0 1.0 copy-start.31
  124.8 0.9 copy-start.21
  124.8 0.9 copy-start.23
  124.8 0.9 copy-start.24
  124.8 1.0 copy-start.25
  124.8 1.0 copy-start.26
  124.8 1.0 copy-start.27
  124.8 1.0 copy-start.28
  125.7 0.9 copy-start.29
